TPU v7x, 256 devices: a whole 4x4x8 slice. The times are simulated.
256 devices in a mesh: dp: 2 (over z_lo), expert: 32 (over y, z_hi, core), tensor: 4 (over x).
Axes of the slice: x: 4, y: 4, z: 8 (z_hi: 4, z_lo: 2; z = z_hi * 2 + z_lo), core: 2. Of those that a mesh axis runs over, the one named last changes fastest.
Arguments:
- context: bfloat16 [8192, 2048], P(('dp', 'expert'), 'tensor'), may hold values from -6 to 6
- residual: bfloat16 [8192, 2048], P(('dp', 'expert')), may hold values from -6 to 6
- wo_rows: bfloat16 [2048, 2048], P('tensor'), may hold values from -0.125 to 0.125
- norm_gain: float32 [2048], replicated, may hold values from 0.25 to 1.75
- analyzer_out: bfloat16 [8192, 2048], P(('dp', 'expert'), 'tensor'), may hold values from -6 to 6
- gate_probs: float32 [8192, 6], P(('dp', 'expert')), may hold values from 0.05 to 0.5
- expert_ids: int32 [8192, 6], P(('dp', 'expert')), may hold values from 0 to 63, all different within a row; in each aligned block of 128 rows (0 to 127, 128 to 255, ...) at most 14 rows name the same one
- w_gate_up: bfloat16 [64, 2, 2048, 1408], P('expert', None, 'dp', 'tensor'), may hold values from -0.125 to 0.125
- w_down: bfloat16 [64, 1408, 2048], P('expert', 'tensor', 'dp'), may hold values from -0.15625 to 0.15625
Outputs:
- block_out: bfloat16 [8192, 2048], P(('dp', 'expert'), 'tensor')
- context_grad: bfloat16 [8192, 2048], P(('dp', 'expert'), 'tensor')
- gate_prob_grad: float32 [8192, 6], P(('dp', 'expert'))
- gate_up_grad: bfloat16 [64, 2, 2048, 1408], P('expert', None, 'dp', 'tensor')
- down_grad: bfloat16 [64, 1408, 2048], P('expert', 'tensor', 'dp')
Inputs may be any that keep to these rules, and one draw needn't show every extreme that they name: `expert_ids`: each row names 6 different experts; within each device's rows (aligned blocks of 128 rows) no expert is named more than 14 times, a bound that some block reaches.
All inputs are finite; a program needn't handle non-finite values.
Results may differ from a plain program's by a relative error of at most 0.024.
Values may be sent and summed in bfloat16 or wider, within the bound.
No kernel may reach another device: no remote copies, remote signals or barrier semaphores. Data moves between devices by JAX's collectives and lax.ppermute only.
A program may use at most 128 MiB of HBM per device.

v0:
```python
import jax
import jax.numpy as jnp
from jax import lax
from jax.sharding import PartitionSpec as P

EXPERTS = 64
CAP = 14
NORM_EPS = 1e-06
LOSS_WEIGHT = 0.25


def to_experts(outgoing):
    return lax.all_to_all(outgoing, "expert", split_axis=1, concat_axis=1, tiled=True)


def to_tokens(outgoing):
    return lax.all_to_all(outgoing, "expert", split_axis=1, concat_axis=1, tiled=True)


DP_SWAP = [(0, 1), (1, 0)]


def tensor_shift(value, shift, count):
    return lax.ppermute(value, "tensor", [(j, (j + shift) % count) for j in range(count)])


def by_source(received, count):
    order = (lax.axis_index("tensor") - jnp.arange(count)) % count
    return jnp.take(jnp.stack(received), order, axis=0)


def tensor_pieces(value):
    count = lax.axis_size("tensor")
    received = [value] + [tensor_shift(value, shift, count) for shift in range(1, count)]
    return by_source(received, count)


def tensor_total(value):
    pieces = tensor_pieces(value)
    total = pieces[0]
    for member in range(1, pieces.shape[0]):
        total = total + pieces[member]
    return total


def tensor_scattered(value):
    count = lax.axis_size("tensor")
    width = value.shape[1] // count
    me = lax.axis_index("tensor")
    received = [lax.dynamic_slice_in_dim(value, me * width, width, 1)]
    for shift in range(1, count):
        sent = lax.dynamic_slice_in_dim(value, (me + shift) % count * width, width, 1)
        received.append(tensor_shift(sent, shift, count))
    pieces = by_source(received, count).astype(jnp.float32)
    total = pieces[0]
    for member in range(1, count):
        total = total + pieces[member]
    return total


def dp_joined(own, dp_first, axis):
    other = lax.ppermute(own, "dp", DP_SWAP)
    return jnp.where(
        dp_first, jnp.concatenate([own, other], axis=axis), jnp.concatenate([other, own], axis=axis)
    )


def dp_halves_sent(part, dp_first, axis):
    half = part.shape[axis] // 2
    low = lax.slice_in_dim(part, 0, half, axis=axis).astype(jnp.bfloat16)
    high = lax.slice_in_dim(part, half, 2 * half, axis=axis).astype(jnp.bfloat16)
    kept = jnp.where(dp_first, low, high)
    arrived = lax.ppermute(jnp.where(dp_first, high, low), "dp", DP_SWAP)
    return (kept, arrived)


def halves_added(kept, arrived):
    return (kept.astype(jnp.float32) + arrived.astype(jnp.float32)).astype(jnp.bfloat16)


def weight_terms(arrived, activation, grad_in, d_gate_pre, d_up_pre):
    down_part = jnp.einsum(
        "escf,escd->efd", activation, grad_in, preferred_element_type=jnp.float32
    )
    gate_part = jnp.einsum(
        "escd,escf->edf", arrived, d_gate_pre, preferred_element_type=jnp.float32
    )
    up_part = jnp.einsum("escd,escf->edf", arrived, d_up_pre, preferred_element_type=jnp.float32)
    return (jnp.stack([gate_part, up_part], axis=1), down_part)


def per_device(
    context, residual, wo_rows, norm_gain, analyzer_out, gate_probs, expert_ids, w_gate_up, w_down
):
    tok_count, top_count = expert_ids.shape
    feature_count = residual.shape[1]
    tensor_count = lax.axis_size("tensor")
    expert_ranks = lax.axis_size("expert")
    col_count = feature_count // tensor_count
    col_start = lax.axis_index("tensor") * col_count
    local_experts = w_gate_up.shape[0]
    slot_count = EXPERTS * CAP
    expert_range = jnp.arange(EXPERTS, dtype=jnp.int32)
    slot_order = expert_range % local_experts * expert_ranks + expert_range // local_experts
    dp_first = lax.axis_index("dp") == 0
    down_other = lax.ppermute(w_down, "dp", DP_SWAP)
    partial_attn = jnp.dot(context, wo_rows, preferred_element_type=jnp.float32)
    attn_cols = tensor_scattered(partial_attn.astype(jnp.bfloat16))
    hidden_cols = (
        lax.dynamic_slice_in_dim(residual, col_start, col_count, 1).astype(jnp.float32) + attn_cols
    )
    square_sum = tensor_total(jnp.sum(hidden_cols * hidden_cols, axis=1, keepdims=True))
    inv_rms = lax.rsqrt(square_sum / feature_count + NORM_EPS)
    gain_cols = lax.dynamic_slice_in_dim(norm_gain, col_start, col_count, 0)
    normed = (gain_cols * hidden_cols * inv_rms).astype(jnp.bfloat16)
    flat_ids = expert_ids.reshape(-1)
    onehot = (flat_ids[:, None] == expert_range[None, :]).astype(jnp.int32)
    slot_index = jnp.sum((jnp.cumsum(onehot, axis=0) - onehot) * onehot, axis=1)
    expert_slot = jnp.sum(onehot * slot_order[None, :], axis=1)
    dest_row = expert_slot * CAP + slot_index
    sentinel = tok_count * top_count
    row_entry = (
        jnp.full((slot_count,), sentinel, jnp.int32)
        .at[dest_row]
        .set(jnp.arange(sentinel, dtype=jnp.int32))
    )
    row_token = row_entry // top_count
    gate_pad = jnp.concatenate([gate_probs.reshape(-1), jnp.zeros((1,), jnp.float32)])
    row_gate = gate_pad[row_entry]
    normed_pad = jnp.concatenate([normed, jnp.zeros((1, col_count), jnp.bfloat16)], axis=0)
    outgoing = normed_pad[row_token].reshape(local_experts, expert_ranks, CAP, col_count)
    first_other = lax.ppermute(w_gate_up[0:1, 0:1], "dp", DP_SWAP)
    down_other, first_other, outgoing = lax.optimization_barrier(
        (down_other, first_other, outgoing)
    )
    second_other = lax.ppermute(w_gate_up[0:1, 1:2], "dp", DP_SWAP)
    rest_other = lax.ppermute(w_gate_up[1:], "dp", DP_SWAP)
    gate_up_other = jnp.concatenate(
        [jnp.concatenate([first_other, second_other], axis=1), rest_other], axis=0
    )
    gate_up_full = jnp.where(
        dp_first,
        jnp.concatenate([w_gate_up, gate_up_other], axis=2),
        jnp.concatenate([gate_up_other, w_gate_up], axis=2),
    )
    down_full = jnp.where(
        dp_first,
        jnp.concatenate([w_down, down_other], axis=2),
        jnp.concatenate([down_other, w_down], axis=2),
    )
    arrived = lax.all_gather(to_experts(outgoing), "tensor", axis=3, tiled=True)
    gate_full = gate_up_full[:, 0]
    up_full = gate_up_full[:, 1]
    half_count = feature_count // 2
    dp_index = lax.axis_index("dp")
    own_rows = lax.dynamic_slice_in_dim(arrived, dp_index * half_count, half_count, 3)
    other_rows = lax.dynamic_slice_in_dim(arrived, (1 - dp_index) * half_count, half_count, 3)
    other_pieces = ((first_other[0, 0], second_other[0, 0]), (rest_other[0, 0], rest_other[0, 1]))

    def projected(which):
        return jnp.stack(
            [
                jnp.einsum(
                    "scd,df->scf",
                    own_rows[e],
                    w_gate_up[e, which],
                    preferred_element_type=jnp.float32,
                )
                + jnp.einsum(
                    "scd,df->scf",
                    other_rows[e],
                    other_pieces[e][which],
                    preferred_element_type=jnp.float32,
                )
                for e in range(local_experts)
            ]
        )

    pre_gate = projected(0)
    pre_up = projected(1)
    activation = (jax.nn.silu(pre_gate) * pre_up).astype(jnp.bfloat16)
    partial_out = jnp.einsum(
        "escf,efd->escd", activation, down_full, preferred_element_type=jnp.float32
    )
    summed_out = lax.psum_scatter(
        partial_out.astype(jnp.bfloat16), "tensor", scatter_dimension=3, tiled=True
    )
    returned = to_tokens(summed_out).reshape(slot_count, col_count)
    entry_out = returned[dest_row].reshape(tok_count, top_count, col_count).astype(jnp.float32)
    block_out = (hidden_cols + jnp.sum(gate_probs[:, :, None] * entry_out, axis=1)).astype(
        jnp.bfloat16
    )
    error = (
        LOSS_WEIGHT * (block_out.astype(jnp.float32) - analyzer_out.astype(jnp.float32))
    ).astype(jnp.bfloat16)
    gate_partial = jnp.sum(error.astype(jnp.float32)[:, None, :] * entry_out, axis=2)
    error_pad = jnp.concatenate([error, jnp.zeros((1, col_count), jnp.bfloat16)], axis=0)
    grad_slot = (row_gate[:, None] * error_pad[row_token].astype(jnp.float32)).astype(jnp.bfloat16)
    grad_slot = grad_slot.reshape(local_experts, expert_ranks, CAP, col_count)
    grad_in = lax.all_gather(to_experts(grad_slot), "tensor", axis=3, tiled=True)
    d_act = jnp.einsum("escd,efd->escf", grad_in, down_full, preferred_element_type=jnp.float32)
    sigmoid_pre = jax.nn.sigmoid(pre_gate)
    d_gate_pre = (d_act * pre_up * sigmoid_pre * (1.0 + pre_gate * (1.0 - sigmoid_pre))).astype(
        jnp.bfloat16
    )
    d_up_pre = (d_act * pre_gate * sigmoid_pre).astype(jnp.bfloat16)
    d_entry_part = jnp.einsum(
        "escf,edf->escd", d_gate_pre, gate_full, preferred_element_type=jnp.float32
    )
    d_entry_part = d_entry_part + jnp.einsum(
        "escf,edf->escd", d_up_pre, up_full, preferred_element_type=jnp.float32
    )
    d_entry_sum = lax.psum_scatter(
        d_entry_part.astype(jnp.bfloat16), "tensor", scatter_dimension=3, tiled=True
    )
    d_returned = to_tokens(d_entry_sum).reshape(slot_count, col_count)
    d_normed = jnp.sum(
        d_returned[dest_row].reshape(tok_count, top_count, col_count).astype(jnp.float32), axis=1
    )
    scaled = gain_cols * d_normed
    norm_partial = jnp.sum(scaled * hidden_cols, axis=1)
    norm_dots, gate_prob_grad = lax.psum((norm_partial, gate_partial), "tensor")
    cubed = inv_rms * inv_rms * inv_rms
    d_hidden = (
        error.astype(jnp.float32)
        + inv_rms * scaled
        - hidden_cols * cubed * norm_dots[:, None] / feature_count
    ).astype(jnp.bfloat16)
    context_grad = lax.dot_general(
        lax.all_gather(d_hidden, "tensor", axis=1, tiled=True),
        wo_rows,
        (((1,), (1,)), ((), ())),
        preferred_element_type=jnp.float32,
    ).astype(jnp.bfloat16)
    gate_up_part, down_part = weight_terms(arrived, activation, grad_in, d_gate_pre, d_up_pre)
    gate_up_kept, gate_up_arrived = dp_halves_sent(gate_up_part, dp_first, 2)
    down_kept, down_arrived = dp_halves_sent(down_part, dp_first, 2)
    gate_up_arrived, down_arrived, context_grad = lax.optimization_barrier(
        (gate_up_arrived, down_arrived, context_grad)
    )
    return (
        block_out,
        context_grad,
        gate_prob_grad,
        halves_added(gate_up_kept, gate_up_arrived),
        halves_added(down_kept, down_arrived),
    )


def solution(mesh):
    in_specs = (
        P(("dp", "expert"), "tensor"),
        P(("dp", "expert"), None),
        P("tensor", None),
        P(),
        P(("dp", "expert"), "tensor"),
        P(("dp", "expert"), None),
        P(("dp", "expert"), None),
        P("expert", None, "dp", "tensor"),
        P("expert", "tensor", "dp"),
    )
    out_specs = (
        P(("dp", "expert"), "tensor"),
        P(("dp", "expert"), "tensor"),
        P(("dp", "expert"), None),
        P("expert", None, "dp", "tensor"),
        P("expert", "tensor", "dp"),
    )
    return jax.shard_map(
        per_device, mesh=mesh, in_specs=in_specs, out_specs=out_specs, check_vma=False
    )
```

profile of v0, /device:TPU:32, one launch (start us, length us, event | category | flops | bytes accessed | tf_op | source)
XLA Modules:
  0.0 521.8 jit_solution(2365264565536121640)
XLA Ops:
  12.5 2.7 collective-permute-start.1
  22.7 3.4 scatter_custom_fusion
  37.5 4.0 gather_fusion.2
  43.6 22.6 %collective-permute-done.3 = bf16[2,352,1024]{2,1,0:T(8,128)(2,1)} collective-permute-done((bf16[2,352,1024]{2,1,0:T(8,128)(2,1)}, bf16[2,352,1024]{2,1,0:T(8,128)(2,1)}, u32[]{:S(2)}, u32[]{:S(2)}) %collective-permute-start.3) | collective-permute-done | bytes 1441824 | tf_op jit(solution)/shard_map/ppermute | solution.py:106
  68.3 36.9 %all_to_all.20 = bf16[2,32,14,512]{3,0,2,1:T(2,128)(2,1)S(1)} all-to-all(bf16[2,32,14,512]{3,0,2,1:T(2,128)(2,1)S(1)} %copy.62), channel_id=1, replica_groups=mesh['dp'=2,'expert'=32,'tensor'=4] {'expert'}, dimensions={1} | all-to-all | bytes 1835008 | tf_op jit(solution)/shard_map/all_to_all | solution.py:13
  106.4 2.6 slice.107
  111.2 36.1 %all-gather.3.cloned.1.call-done = bf16[2,32,14,2048]{3,1,2,0:T(8,128)(2,1)} async-done(((bf16[2,32,14,512]{3,1,2,0:T(8,128)(2,1)}), bf16[2,32,14,2048]{3,1,2,0:T(8,128)(2,1)}) %all-gather.3.cloned.1.call-update) | async-done | bytes 3670032 | tf_op jit(solution)/shard_map/all_gather | solution.py:151
  162.5 7.0 %convolution_convert_fusion = bf16[2,32,14,2048]{3,1,2,0:T(8,128)(2,1)} fusion(bf16[2,32,14,352]{3,1,2,0:T(8,128)(2,1)S(1)} %multiply_convert_fusion.3, bf16[2,352,1024]{2,1,0:T(8,128)(2,1)} %collective-permute-done.3, bf16[2,352,1024]{2,1,0:T(8,128)(2,1)} %param.17, pred[]{:T(512)S(6)} %eq.45), kind=kOutput, calls=%fused_computation.15 | convolution fusion | flops 1306656768 | bytes 7184385 | tf_op jit(solution)/shard_map/escf,efd->escd/dot_general | solution.py:182
  169.5 45.5 %reduce-scatter.3.cloned.1.call-done = bf16[2,32,14,512]{3,1,2,0:T(8,128)(2,1)} async-done(((bf16[2,32,14,2048]{3,1,2,0:T(8,128)(2,1)}), bf16[2,32,14,512]{3,1,2,0:T(8,128)(2,1)}) %reduce-scatter.3.cloned.1.call-update) | async-done | bytes 917520 | tf_op jit(solution)/shard_map/reduce_scatter | solution.py:185
  215.1 3.0 copy.64
  218.1 9.1 %all-to-all-start.1 = ((bf16[2,32,14,512]{3,0,2,1:T(2,128)(2,1)}), bf16[2,32,14,512]{3,0,2,1:T(2,128)(2,1)}, u32[]{:S(2)}, u32[]{:S(2)}) async-start(bf16[2,32,14,512]{3,0,2,1:T(2,128)(2,1)} %copy.64), calls=%async_computation.2 | async-start | bytes 1835008 | tf_op jit(solution)/shard_map/all_to_all | solution.py:17
  227.7 3.7 gather_fusion.4
  231.5 19.0 %all-to-all-done.1 = bf16[2,32,14,512]{3,0,2,1:T(2,128)(2,1)} async-done(((bf16[2,32,14,512]{3,0,2,1:T(2,128)(2,1)}), bf16[2,32,14,512]{3,0,2,1:T(2,128)(2,1)}, u32[]{:S(2)}, u32[]{:S(2)}) %all-to-all-start.1) | async-done | bytes 917536 | tf_op jit(solution)/shard_map/all_to_all | solution.py:17
  254.3 3.3 gather_fusion.3
  263.3 4.0 gather_fusion.5
  272.5 30.2 %all_to_all.21 = bf16[2,32,14,512]{3,0,2,1:T(2,128)(2,1)S(1)} all-to-all(bf16[2,32,14,512]{3,0,2,1:T(2,128)(2,1)S(1)} %copy.67), channel_id=1, replica_groups=mesh['dp'=2,'expert'=32,'tensor'=4] {'expert'}, dimensions={1} | all-to-all | bytes 1835008 | tf_op jit(solution)/shard_map/all_to_all | solution.py:13
  304.2 7.6 %maximum_select_fusion = bf16[2,2,2048,352]{2,3,1,0:T(8,128)(2,1)} fusion(bf16[1,2,1024,352]{2,3,1,0:T(8,128)(2,1)} %collective-permute-done.8, bf16[1,1,1024,352]{2,3,1,0:T(8,128)(2,1)} %collective-permute-done.9, bf16[1,1,1024,352]{2,3,1,0:T(8,128)(2,1)S(1)} %copy-done.11, bf16[2,2,1024,352]{2,3,1,0:T(8,128)(2,1)} %param.16, pred[]{:T(512)S(6)} %eq.45), kind=kLoop, calls=%fused_computation.10 | loop fusion | flops 49020928 | bytes 11534337 | tf_op jit(solution)/shard_map/jit(_where)/select_n | solution.py:141
  311.8 38.6 %all-gather.5.cloned.1.call-done = bf16[2,32,14,2048]{3,1,2,0:T(8,128)(2,1)} async-done(((bf16[2,32,14,512]{3,1,2,0:T(8,128)(2,1)}), bf16[2,32,14,2048]{3,1,2,0:T(8,128)(2,1)}) %all-gather.5.cloned.1.call-update) | async-done | bytes 3670032 | tf_op jit(solution)/shard_map/all_gather | solution.py:200
  350.3 7.0 %multiply_convert_fusion.2 = (bf16[2,32,14,352]{3,1,2,0:T(8,128)(2,1)S(1)}, bf16[2,32,14,352]{3,1,2,0:T(8,128)(2,1)S(1)}) fusion(f32[1,32,14,352]{3,1,2,0:T(8,128)} %copy-done.14, f32[1,32,14,352]{3,1,2,0:T(8,128)} %copy-done.15, f32[1,32,14,352]{3,1,2,0:T(8,128)} %copy-done.13, f32[1,32,14,352]{3,1,2,0:T(8,128)} %copy-done.12, ...), kind=kOutput, calls=%fused_computation.32 | convolution fusion | flops 1309552640 | bytes 10338305 | tf_op jit(solution)/shard_map/escd,efd->escf/dot_general | solution.py:201
  359.5 3.9 add_convert_fusion
  363.5 3.9 convolution_bitcast_fusion.1
  373.6 35.4 %reduce-scatter.5.cloned.1.call-done = bf16[2,32,14,512]{3,1,2,0:T(8,128)(2,1)} async-done(((bf16[2,32,14,2048]{3,1,2,0:T(8,128)(2,1)}), bf16[2,32,14,512]{3,1,2,0:T(8,128)(2,1)}) %reduce-scatter.5.cloned.1.call-update) | async-done | bytes 917520 | tf_op jit(solution)/shard_map/reduce_scatter | solution.py:213
  409.0 3.1 copy.69
  412.1 8.9 %all-to-all-start.3 = ((bf16[2,32,14,512]{3,0,2,1:T(2,128)(2,1)}), bf16[2,32,14,512]{3,0,2,1:T(2,128)(2,1)S(1)}, u32[]{:S(2)}, u32[]{:S(2)}) async-start(bf16[2,32,14,512]{3,0,2,1:T(2,128)(2,1)} %copy.69), calls=%async_computation.5 | async-start | bytes 1835008 | tf_op jit(solution)/shard_map/all_to_all | solution.py:17
  421.0 4.0 bitcast_convert_fusion
  429.6 31.2 %all-to-all-done.3 = bf16[2,32,14,512]{3,0,2,1:T(2,128)(2,1)S(1)} async-done(((bf16[2,32,14,512]{3,0,2,1:T(2,128)(2,1)}), bf16[2,32,14,512]{3,0,2,1:T(2,128)(2,1)S(1)}, u32[]{:S(2)}, u32[]{:S(2)}) %all-to-all-start.3) | async-done | bytes 917536 | tf_op jit(solution)/shard_map/all_to_all | solution.py:17
  463.4 3.3 gather_fusion.6
  466.7 2.6 reshape.264
  471.6 16.2 %all-reduce.2 = (f32[128]{0:T(128)S(1)}, f32[128,6]{1,0:T(8,128)S(1)}) all-reduce(f32[128]{0:T(128)S(1)} %multiply_reduce_fusion.2, f32[128,6]{1,0:T(8,128)S(1)} %multiply_reduce_fusion), channel_id=1, replica_groups=mesh['dp'=2,'expert'=32,'tensor'=4] {'tensor'}, use_global_device_ids=true, to_apply=%region_11.12 | all-reduce | flops 896 | bytes 7168 | tf_op jit(solution)/shard_map/psum | solution.py:222
  488.0 13.6 %all_gather.11 = bf16[128,2048]{1,0:T(8,128)(2,1)S(1)} all-gather(bf16[128,512]{1,0:T(8,128)(2,1)S(1)} %subtract_convert_fusion), channel_id=1, replica_groups=mesh['dp'=2,'expert'=32,'tensor'=4] {'tensor'}, dimensions={1}, use_global_device_ids=true | all-gather | bytes 655360 | tf_op jit(solution)/shard_map/all_gather | solution.py:230
  503.1 3.4 add_convert_fusion.2
  506.5 5.7 %add_convert_fusion.1 = bf16[2,2,1024,352]{2,3,0,1:T(8,128)(2,1)S(1)} fusion(bf16[2,2,1024,352]{2,3,0,1:T(8,128)(2,1)} %collective-permute-done.10, pred[]{:T(512)S(6)} %eq.45, bf16[2,2,2048,352]{2,3,0,1:T(8,128)(2,1)} %copy-done.1), kind=kLoop, calls=%fused_computation.12 | loop fusion | flops 7208960 | bytes 11534337 | tf_op jit(solution)/shard_map/convert_element_type | solution.py:78
  (148 shorter events, 85.5 us)
Async XLA Ops:
  7.2 140.1 %all-gather.3.cloned.1.call-start = ((), (), s32[]{:S(2)}) async-start(), calls=%async_computation.6 | async-start | bytes 4587520 | tf_op jit(solution)/shard_map/all_gather | solution.py:151
  8.8 7.9 %copy-start.6 = (bf16[2,2,1024,352]{2,3,1,0:T(8,128)(2,1)S(1)}, bf16[2,2,1024,352]{2,3,1,0:T(8,128)(2,1)}, u32[]{:S(2)}) copy-start(bf16[2,2,1024,352]{2,3,1,0:T(8,128)(2,1)} %param.16) | copy-start | bytes 8650756
  8.8 11.2 %copy-start.21 = (s32[128,6]{0,1:T(8,128)S(1)}, s32[128,6]{0,1:T(8,128)}, u32[]{:S(2)}) copy-start(s32[128,6]{0,1:T(8,128)} %param.15) | copy-start | bytes 9220
  11.0 15.1 %collective-permute-start = (bf16[128,512]{1,0:T(8,128)(2,1)}, bf16[128,512]{1,0:T(8,128)(2,1)}, u32[]{:S(2)}, u32[]{:S(2)}) collective-permute-start(bf16[128,512]{1,0:T(8,128)(2,1)} %get-tuple-element.55), channel_id=1, source_target_pairs={{0,1},{1,2},{2,3},{3,0},{4,5},{5,6},{6,7},{7,4},{8,9},{9,10},{10,1... | collective-permute-start | bytes 393224 | tf_op jit(solution)/shard_map/ppermute | solution.py:24
  12.5 13.6 %collective-permute-start.1 = (bf16[128,512]{1,0:T(8,128)(2,1)}, bf16[128,512]{1,0:T(8,128)(2,1)}, u32[]{:S(2)}, u32[]{:S(2)}) collective-permute-start(bf16[128,512]{1,0:T(8,128)(2,1)} %get-tuple-element.54), channel_id=1, source_target_pairs={{0,2},{1,3},{2,0},{3,1},{4,6},{5,7},{6,4},{7,5},{8,10},{9,11},{10,... | collective-permute-start | bytes 393224 | tf_op jit(solution)/shard_map/ppermute | solution.py:24
  15.3 10.9 %collective-permute-start.2 = (bf16[128,512]{1,0:T(8,128)(2,1)S(1)}, bf16[128,512]{1,0:T(8,128)(2,1)}, u32[]{:S(2)}, u32[]{:S(2)}) collective-permute-start(bf16[128,512]{1,0:T(8,128)(2,1)S(1)} %get-tuple-element.53), channel_id=1, source_target_pairs={{0,3},{1,0},{2,1},{3,2},{4,7},{5,4},{6,5},{7,6},{8,11},{9,8},{10,9... | collective-permute-start | bytes 393224 | tf_op jit(solution)/shard_map/ppermute | solution.py:24
  17.9 25.7 %collective-permute-start.4 = (bf16[1,1,1024,352]{2,3,1,0:T(8,128)(2,1)}, bf16[1,1,1024,352]{2,3,1,0:T(8,128)(2,1)S(1)}, u32[]{:S(2)}, u32[]{:S(2)}) collective-permute-start(bf16[1,1,1024,352]{2,3,1,0:T(8,128)(2,1)} %get-tuple-element.49), channel_id=1, source_target_pairs={{0,128},{128,0},{1,129},{129,1},{2,130},{130,2},{3,131},{131,3},{4... | collective-permute-start | bytes 2162696 | tf_op jit(solution)/shard_map/ppermute | solution.py:132
  18.0 48.1 %collective-permute-start.3 = (bf16[2,352,1024]{2,1,0:T(8,128)(2,1)}, bf16[2,352,1024]{2,1,0:T(8,128)(2,1)}, u32[]{:S(2)}, u32[]{:S(2)}) collective-permute-start(bf16[2,352,1024]{2,1,0:T(8,128)(2,1)} %param.17), channel_id=1, source_target_pairs={{0,128},{128,0},{1,129},{129,1},{2,130},{130,2},{3,131},{131,3},{4... | collective-permute-start | bytes 4325384 | tf_op jit(solution)/shard_map/ppermute | solution.py:106
  31.0 4.8 collective-permute-start.5
  31.6 5.1 collective-permute-start.6
  32.5 4.2 collective-permute-start.7
  43.6 105.8 %copy-start.10 = (bf16[1,1,1024,352]{2,3,1,0:T(8,128)(2,1)}, bf16[1,1,1024,352]{2,3,1,0:T(8,128)(2,1)S(1)}, u32[]{:S(2)}) copy-start(bf16[1,1,1024,352]{2,3,1,0:T(8,128)(2,1)S(1)} %collective-permute-done.4) | copy-start | bytes 2162692
  106.4 108.7 %reduce-scatter.3.cloned.1.call-start = ((), (), s32[]{:S(2)}) async-start(), calls=%async_computation.7 | async-start | bytes 4587520 | tf_op jit(solution)/shard_map/reduce_scatter | solution.py:185
  109.0 44.6 %collective-permute-start.8 = (bf16[1,2,1024,352]{2,3,1,0:T(8,128)(2,1)}, bf16[1,2,1024,352]{2,3,1,0:T(8,128)(2,1)}, u32[]{:S(2)}, u32[]{:S(2)}) collective-permute-start(bf16[1,2,1024,352]{2,3,1,0:T(8,128)(2,1)} %slice.107), channel_id=1, source_target_pairs={{0,128},{128,0},{1,129},{129,1},{2,130},{130,2},{3,131},{131,3},{4... | collective-permute-start | bytes 4325384 | tf_op jit(solution)/shard_map/ppermute | solution.py:137
  109.9 48.6 %collective-permute-start.9 = (bf16[1,1,1024,352]{2,3,1,0:T(8,128)(2,1)}, bf16[1,1,1024,352]{2,3,1,0:T(8,128)(2,1)}, u32[]{:S(2)}, u32[]{:S(2)}) collective-permute-start(bf16[1,1,1024,352]{2,3,1,0:T(8,128)(2,1)} %get-tuple-element.48), channel_id=1, source_target_pairs={{0,128},{128,0},{1,129},{129,1},{2,130},{130,2},{3,131},{131,3},{4... | collective-permute-start | bytes 2162696 | tf_op jit(solution)/shard_map/ppermute | solution.py:136
  147.3 4.2 copy-start.7
  149.5 4.1 copy-start.8
  151.5 8.8 %copy-start.12 = (f32[1,32,14,352]{3,1,2,0:T(8,128)}, f32[1,32,14,352]{3,1,2,0:T(8,128)S(1)}, u32[]{:S(2)}) copy-start(f32[1,32,14,352]{3,1,2,0:T(8,128)S(1)} %fusion.8) | copy-start | bytes 1892356
  155.4 4.9 copy-start.13
  169.5 57.9 %copy-start.22 = (f32[128,6]{0,1:T(8,128)S(1)}, f32[128,6]{0,1:T(8,128)}, u32[]{:S(2)}) copy-start(f32[128,6]{0,1:T(8,128)} %param.14) | copy-start | bytes 9220
  218.1 32.4 %all-to-all-start.1 = ((bf16[2,32,14,512]{3,0,2,1:T(2,128)(2,1)}), bf16[2,32,14,512]{3,0,2,1:T(2,128)(2,1)}, u32[]{:S(2)}, u32[]{:S(2)}) async-start(bf16[2,32,14,512]{3,0,2,1:T(2,128)(2,1)} %copy.64), calls=%async_computation.2 | async-start | bytes 1835008 | tf_op jit(solution)/shard_map/all_to_all | solution.py:17
  227.2 123.2 %all-gather.5.cloned.1.call-start = ((), (), s32[]{:S(2)}) async-start(), calls=%async_computation.8 | async-start | bytes 4587520 | tf_op jit(solution)/shard_map/all_gather | solution.py:200
  257.6 4.8 copy-start.20
  271.6 32.7 %copy-start.11 = (bf16[1,1,1024,352]{2,3,1,0:T(8,128)(2,1)S(1)}, bf16[1,1,1024,352]{2,3,1,0:T(8,128)(2,1)}, u32[]{:S(2)}) copy-start(bf16[1,1,1024,352]{2,3,1,0:T(8,128)(2,1)} %copy-done.10) | copy-start | bytes 2162692
  303.9 105.1 %reduce-scatter.5.cloned.1.call-start = ((), (), s32[]{:S(2)}) async-start(), calls=%async_computation.9 | async-start | bytes 4587520 | tf_op jit(solution)/shard_map/reduce_scatter | solution.py:213
  350.3 7.1 %copy-start.2 = (bf16[2,2,2048,352]{2,3,1,0:T(8,128)(2,1)S(1)}, bf16[2,2,2048,352]{2,3,1,0:T(8,128)(2,1)}, u32[]{:S(2)}) copy-start(bf16[2,2,2048,352]{2,3,1,0:T(8,128)(2,1)} %maximum_select_fusion) | copy-start | bytes 17301508
  363.5 3.9 copy-start.9
  363.5 3.9 copy-start.19
  373.1 130.0 %collective-permute-start.10 = (bf16[2,2,1024,352]{2,3,0,1:T(8,128)(2,1)}, bf16[2,2,1024,352]{2,3,0,1:T(8,128)(2,1)}, u32[]{:S(2)}, u32[]{:S(2)}) collective-permute-start(bf16[2,2,1024,352]{2,3,0,1:T(8,128)(2,1)} %broadcast_select_fusion), channel_id=1, source_target_pairs={{0,128},{128,0},{1,129},{129,1},{2,130},{130,2},{3,131},{131,3},{4... | collective-permute-start | bytes 8650760 | tf_op jit(solution)/shard_map/ppermute | solution.py:73
  412.1 48.7 %all-to-all-start.3 = ((bf16[2,32,14,512]{3,0,2,1:T(2,128)(2,1)}), bf16[2,32,14,512]{3,0,2,1:T(2,128)(2,1)S(1)}, u32[]{:S(2)}, u32[]{:S(2)}) async-start(bf16[2,32,14,512]{3,0,2,1:T(2,128)(2,1)} %copy.69), calls=%async_computation.5 | async-start | bytes 1835008 | tf_op jit(solution)/shard_map/all_to_all | solution.py:17
  427.8 75.2 %collective-permute-start.11 = (bf16[2,352,1024]{2,1,0:T(8,128)(2,1)}, bf16[2,352,1024]{2,1,0:T(8,128)(2,1)}, u32[]{:S(2)}, u32[]{:S(2)}) collective-permute-start(bf16[2,352,1024]{2,1,0:T(8,128)(2,1)} %broadcast_select_fusion.1), channel_id=1, source_target_pairs={{0,128},{128,0},{1,129},{129,1},{2,130},{130,2},{3,131},{131,3},{4... | collective-permute-start | bytes 4325384 | tf_op jit(solution)/shard_map/ppermute | solution.py:73
  487.8 15.2 %copy-start.5 = (bf16[2,352,2048]{2,1,0:T(8,128)(2,1)S(1)}, bf16[2,352,2048]{2,1,0:T(8,128)(2,1)}, u32[]{:S(2)}) copy-start(bf16[2,352,2048]{2,1,0:T(8,128)(2,1)} %copy-done.4) | copy-start | bytes 8650756
  (9 other events, 18.2 us)
Sparse Core Ops, SparseCore 0:
  106.5 40.7 all-gather.2
  169.6 45.3 reduce-scatter.2
  304.0 46.2 all-gather.4
  363.6 45.3 reduce-scatter.4
where the time goes:
time: 531 us; the launch traced here: 522 us
  waiting for transfers between devices  230 us (43%)
  blocking collectives  96.9 us (18%)
  local copies, waits for them, and re-layouts  66.3 us (12%)
  matrix products  45.5 us (9%)
  other arithmetic  34.5 us (6%)
  starting transfers between devices  33.8 us (6%)
  between operations  14.9 us (3%)
    all_to_all x2, blocking collectives, to_experts(): lax.all_to_all(outgoing, 'expert', split_axis=1, concat_axis=1, tiled=True)  67.1 us
    all_to_all x2, waiting for transfers between devices, to_tokens(): lax.all_to_all(outgoing, 'expert', split_axis=1, concat_axis=1, tiled=True)  50.2 us
    reduce_scatter x1, waiting for transfers between devices, per_device(): lax.psum_scatter(partial_out.astype(jnp.bfloat16), 'tensor', scatter_dime...  45.5 us
    all_gather x1, waiting for transfers between devices, per_device(): lax.all_gather(to_experts(grad_slot), 'tensor', axis=3, tiled=True)  38.6 us
    all_gather x1, waiting for transfers between devices, per_device(): arrived = lax.all_gather(to_experts(outgoing), 'tensor', axis=3, tiled=True)  36.1 us
    reduce_scatter x1, waiting for transfers between devices, per_device(): lax.psum_scatter(d_entry_part.astype(jnp.bfloat16), 'tensor', scatter_dim...  35.4 us
    ppermute x1, waiting for transfers between devices, per_device(): down_other = lax.ppermute(w_down, 'dp', DP_SWAP)  22.6 us
    all_to_all x2, starting transfers between devices, to_tokens(): lax.all_to_all(outgoing, 'expert', split_axis=1, concat_axis=1, tiled=True)  18 us
  transfers between devices with their start and end apart: 18, of which 9 were waited for; matrix products, arithmetic and copies ran while one was open for 14% of the time, Pallas kernels for 0%

commit v1 on v0

--- a/solution.py
+++ b/solution.py
@@ -1,3 +1,4 @@
+import functools
 import jax
 import jax.numpy as jnp
 from jax import lax
@@ -7,6 +8,36 @@
 CAP = 14
 NORM_EPS = 1e-06
 LOSS_WEIGHT = 0.25
+
+
+def _begin_side(message, dim_at):
+    w2 = list(message.shape[1:])
+    w2[dim_at] *= message.shape[0]
+    return jnp.moveaxis(message, 0, dim_at).reshape(w2)
+
+
+def watch_the_domain(content, mesh_dim, at_axis):
+    fan = jax.lax.psum(1, mesh_dim)
+    tray = tuple(((m, (m + 1) % fan) for m in range(fan)))
+    ledger = tuple(((w, hop_no) for hop_no, w in tray))
+    b_next, tall = ([], [])
+    t = 0
+    while t < fan - 1:
+        if t % 2 == 0:
+            y1 = jax.lax.ppermute(b_next[-1] if b_next else content, mesh_dim, tray)
+            b_next.append(y1)
+        else:
+            r1 = jax.lax.ppermute(tall[-1] if tall else content, mesh_dim, ledger)
+            tall.append(r1)
+        t = t + 1
+    res = jnp.stack([*b_next[::-1], content, *tall], axis=0)
+    built = jax.lax.axis_index(mesh_dim)
+    far_arr = built - len(b_next)
+    res = res[(jnp.arange(fan) - far_arr) % fan]
+    return _begin_side(res, at_axis)
+
+
+put_axis_part = functools.partial(watch_the_domain, mesh_dim="tensor", at_axis=3)
 
 
 def to_experts(outgoing):
@@ -197,7 +228,7 @@
     error_pad = jnp.concatenate([error, jnp.zeros((1, col_count), jnp.bfloat16)], axis=0)
     grad_slot = (row_gate[:, None] * error_pad[row_token].astype(jnp.float32)).astype(jnp.bfloat16)
     grad_slot = grad_slot.reshape(local_experts, expert_ranks, CAP, col_count)
-    grad_in = lax.all_gather(to_experts(grad_slot), "tensor", axis=3, tiled=True)
+    grad_in = put_axis_part(to_experts(grad_slot))
     d_act = jnp.einsum("escd,efd->escf", grad_in, down_full, preferred_element_type=jnp.float32)
     sigmoid_pre = jax.nn.sigmoid(pre_gate)
     d_gate_pre = (d_act * pre_up * sigmoid_pre * (1.0 + pre_gate * (1.0 - sigmoid_pre))).astype(

time: 531 us -> 571 us (1.075)
  local copies, waits for them, and re-layouts: 66.3 us -> 96.5 us
  waiting for transfers between devices: 230 us -> 219 us
  starting transfers between devices: 33.8 us -> 42.5 us
  other arithmetic: 34.5 us -> 42.4 us
    all_gather x1 -> x0, waiting for transfers between devices: 38.6 us -> none  [per_device(): lax.all_gather(to_experts(grad_slot), 'tensor', axis=3, tiled=True)]
    ppermute x0 -> x3, waiting for transfers between devices: none -> 32.8 us  [the longest x2 32.8 us: watch_the_domain(): y1 = jax.lax.ppermute(b_next[-1] if b_next else content, mesh_dim, tray)]
    gather x0 -> x1, local copies, waits for them, and re-layouts: none -> 11.2 us  [watch_the_domain(): res = res[(jnp.arange(fan) - far_arr) % fan]]
    reduce_scatter x1, waiting for transfers between devices: 35.4 us -> 26.8 us  [per_device(): lax.psum_scatter(d_entry_part.astype(jnp.bfloat16), 'tensor', scatter_dim...]
    another operation x3 -> x4, other arithmetic: 2.35 us -> 9.97 us  [the longest x1 7.62 us: watch_the_domain(): res = jnp.stack([*b_next[::-1], content, *tall], axis=0)]
    reshape x0 -> x1, local copies, waits for them, and re-layouts: none -> 7.36 us  [_begin_side(): return jnp.moveaxis(message, 0, dim_at).reshape(w2)]
    transpose x0 -> x1, local copies, waits for them, and re-layouts: none -> 6.64 us  [_begin_side(): return jnp.moveaxis(message, 0, dim_at).reshape(w2)]
  transfers between devices with their start and end apart: 18 -> 20, of which waited for: 9 -> 10; matrix products, arithmetic and copies ran while one was open for 14% -> 14% of each run, Pallas kernels for 0% -> 0%
where the time goes in v1:
time: 571 us; the launch traced here: 561 us
  waiting for transfers between devices  219 us (38%)
  local copies, waits for them, and re-layouts  96.5 us (17%)
  blocking collectives  95.8 us (17%)
  matrix products  49.2 us (9%)
  starting transfers between devices  42.5 us (7%)
  other arithmetic  42.4 us (7%)
  between operations  14.9 us (3%)
    all_to_all x2, blocking collectives, to_experts(): lax.all_to_all(outgoing, 'expert', split_axis=1, concat_axis=1, tiled=True)  67.1 us
    all_to_all x2, waiting for transfers between devices, to_tokens(): lax.all_to_all(outgoing, 'expert', split_axis=1, concat_axis=1, tiled=True)  53.8 us
    reduce_scatter x1, waiting for transfers between devices, per_device(): lax.psum_scatter(partial_out.astype(jnp.bfloat16), 'tensor', scatter_dime...  45.5 us
    all_gather x1, waiting for transfers between devices, per_device(): arrived = lax.all_gather(to_experts(outgoing), 'tensor', axis=3, tiled=True)  36.1 us
    ppermute x2, waiting for transfers between devices, watch_the_domain(): y1 = jax.lax.ppermute(b_next[-1] if b_next else content, mesh_dim, tray)  32.8 us
    reduce_scatter x1, waiting for transfers between devices, per_device(): lax.psum_scatter(d_entry_part.astype(jnp.bfloat16), 'tensor', scatter_dim...  26.8 us
    ppermute x1, waiting for transfers between devices, per_device(): down_other = lax.ppermute(w_down, 'dp', DP_SWAP)  22.6 us
    all_to_all x2, starting transfers between devices, to_tokens(): lax.all_to_all(outgoing, 'expert', split_axis=1, concat_axis=1, tiled=True)  18.3 us
  transfers between devices with their start and end apart: 20, of which 10 were waited for; matrix products, arithmetic and copies ran while one was open for 14% of the time, Pallas kernels for 0%

profile of v1, /device:TPU:32, one launch (start us, length us, event | category | flops | bytes accessed | tf_op | source)
XLA Modules:
  0.0 560.5 jit_solution(9266879926142511905)
XLA Ops:
  22.7 3.4 scatter_custom_fusion
  37.5 4.0 gather_fusion.2
  43.6 22.6 %collective-permute-done.3 = bf16[2,352,1024]{2,1,0:T(8,128)(2,1)} collective-permute-done((bf16[2,352,1024]{2,1,0:T(8,128)(2,1)}, bf16[2,352,1024]{2,1,0:T(8,128)(2,1)}, u32[]{:S(2)}, u32[]{:S(2)}) %collective-permute-start.3) | collective-permute-done | bytes 1441824 | tf_op jit(solution)/shard_map/ppermute | solution.py:137
  68.3 36.9 %all_to_all.20 = bf16[2,32,14,512]{3,0,2,1:T(2,128)(2,1)S(1)} all-to-all(bf16[2,32,14,512]{3,0,2,1:T(2,128)(2,1)S(1)} %copy.80), channel_id=1, replica_groups=mesh['dp'=2,'expert'=32,'tensor'=4] {'expert'}, dimensions={1} | all-to-all | bytes 1835008 | tf_op jit(solution)/shard_map/all_to_all | solution.py:44
  111.2 36.1 %all-gather.2.cloned.1.call-done = bf16[2,32,14,2048]{3,1,2,0:T(8,128)(2,1)} async-done(((bf16[2,32,14,512]{3,1,2,0:T(8,128)(2,1)}), bf16[2,32,14,2048]{3,1,2,0:T(8,128)(2,1)}) %all-gather.2.cloned.1.call-update) | async-done | bytes 3670032 | tf_op jit(solution)/shard_map/all_gather | solution.py:182
  162.5 6.8 %convolution_convert_fusion = bf16[2,32,14,2048]{3,1,2,0:T(8,128)(2,1)} fusion(bf16[2,32,14,352]{3,1,2,0:T(8,128)(2,1)S(1)} %multiply_convert_fusion.3, bf16[2,352,1024]{2,1,0:T(8,128)(2,1)} %collective-permute-done.3, bf16[2,352,1024]{2,1,0:T(8,128)(2,1)} %param.17, pred[]{:T(512)S(6)} %eq.46), kind=kOutput, calls=%fused_computation.17 | convolution fusion | flops 1306656768 | bytes 7184385 | tf_op jit(solution)/shard_map/escf,efd->escd/dot_general | solution.py:213
  169.3 45.5 %reduce-scatter.3.cloned.1.call-done = bf16[2,32,14,512]{3,1,2,0:T(8,128)(2,1)} async-done(((bf16[2,32,14,2048]{3,1,2,0:T(8,128)(2,1)}), bf16[2,32,14,512]{3,1,2,0:T(8,128)(2,1)}) %reduce-scatter.3.cloned.1.call-update) | async-done | bytes 917520 | tf_op jit(solution)/shard_map/reduce_scatter | solution.py:216
  217.9 9.1 %all-to-all-start.1 = ((bf16[2,32,14,512]{3,0,2,1:T(2,128)(2,1)}), bf16[2,32,14,512]{3,0,2,1:T(2,128)(2,1)}, u32[]{:S(2)}, u32[]{:S(2)}) async-start(bf16[2,32,14,512]{3,0,2,1:T(2,128)(2,1)} %copy.82), calls=%async_computation.2 | async-start | bytes 1835008 | tf_op jit(solution)/shard_map/all_to_all | solution.py:48
  227.7 3.7 gather_fusion.4
  231.6 18.8 %all-to-all-done.1 = bf16[2,32,14,512]{3,0,2,1:T(2,128)(2,1)} async-done(((bf16[2,32,14,512]{3,0,2,1:T(2,128)(2,1)}), bf16[2,32,14,512]{3,0,2,1:T(2,128)(2,1)}, u32[]{:S(2)}, u32[]{:S(2)}) %all-to-all-start.1) | async-done | bytes 917536 | tf_op jit(solution)/shard_map/all_to_all | solution.py:48
  263.1 4.0 gather_fusion.5
  272.3 30.2 %all_to_all.21 = bf16[2,32,14,512]{3,0,2,1:T(2,128)(2,1)S(1)} all-to-all(bf16[2,32,14,512]{3,0,2,1:T(2,128)(2,1)S(1)} %copy.85), channel_id=1, replica_groups=mesh['dp'=2,'expert'=32,'tensor'=4] {'expert'}, dimensions={1} | all-to-all | bytes 1835008 | tf_op jit(solution)/shard_map/all_to_all | solution.py:44
  307.0 20.7 %collective-permute-done.10 = bf16[2,32,14,512]{3,1,2,0:T(8,128)(2,1)} collective-permute-done((bf16[2,32,14,512]{3,1,2,0:T(8,128)(2,1)}, bf16[2,32,14,512]{3,1,2,0:T(8,128)(2,1)}, u32[]{:S(2)}, u32[]{:S(2)}) %collective-permute-start.10) | collective-permute-done | bytes 917536 | tf_op jit(solution)/shard_map/ppermute | solution.py:27
  327.9 7.9 %maximum_select_fusion = bf16[2,2,2048,352]{2,3,1,0:T(8,128)(2,1)} fusion(bf16[1,2,1024,352]{2,3,1,0:T(8,128)(2,1)} %collective-permute-done.8, bf16[1,1,1024,352]{2,3,1,0:T(8,128)(2,1)} %collective-permute-done.9, bf16[1,1,1024,352]{2,3,1,0:T(8,128)(2,1)} %copy-done.9, bf16[2,2,1024,352]{2,3,1,0:T(8,128)(2,1)} %param.16, pred[]{:T(512)S(6)} %eq.46), kind=kLoop, calls=%fused_computation.11 | loop fusion | flops 49020928 | bytes 11534337 | tf_op jit(solution)/shard_map/jit(_where)/select_n | solution.py:172
  338.9 12.1 %collective-permute-done.11 = bf16[2,32,14,512]{3,1,2,0:T(8,128)(2,1)S(1)} collective-permute-done((bf16[2,32,14,512]{3,1,2,0:T(8,128)(2,1)}, bf16[2,32,14,512]{3,1,2,0:T(8,128)(2,1)S(1)}, u32[]{:S(2)}, u32[]{:S(2)}) %collective-permute-start.11) | collective-permute-done | bytes 917536 | tf_op jit(solution)/shard_map/ppermute | solution.py:27
  351.9 7.6 %pad_maximum_fusion = bf16[4,2,32,14,512]{4,1,3,2,0:T(2,128)(2,1)} fusion(bf16[1,2,32,14,512]{4,1,3,2,0:T(2,128)(2,1)S(1)} %bitcast.179, bf16[1,2,32,14,512]{4,1,3,2,0:T(2,128)(2,1)S(1)} %bitcast.177, bf16[1,2,32,14,512]{4,1,3,2,0:T(2,128)(2,1)S(1)} %bitcast.178, bf16[1,2,32,14,512]{4,1,3,2,0:T(2,128)(2,1)S(1)} %bitcast.180), kind=kLoop, calls=%fused_computation.14 | loop fusion | flops 5505024 | bytes 7340032 | tf_op jit(solution)/shard_map/stack | solution.py:33
  359.5 11.2 %gather_fusion.6 = bf16[4,2,32,14,512]{4,1,3,2,0:T(2,128)(2,1)} fusion(bf16[4,2,32,14,512]{4,1,3,2,0:T(2,128)(2,1)} %pad_maximum_fusion, s32[1024]{0:T(1024)S(1)} %pad_clamp_fusion), kind=kCustom, calls=%fused_computation.6 | custom fusion | bytes 7340048 | tf_op jit(solution)/shard_map/gather | solution.py:36
  370.7 6.6 %copy.91 = bf16[2,32,14,4,512]{4,3,1,2,0:T(4,128)(2,1)} copy(bf16[2,32,14,4,512]{4,0,2,1,3:T(2,128)(2,1)} %bitcast.176) | data formatting | bytes 7340032 | tf_op jit(solution)/shard_map/transpose | solution.py:16
  377.3 7.4 %reshape.311 = bf16[2,32,14,2048]{3,1,2,0:T(8,128)(2,1)} reshape(bf16[2,32,14,4,512]{4,3,1,2,0:T(4,128)(2,1)} %copy.91) | data formatting | bytes 7340032 | tf_op jit(solution)/shard_map/reshape | solution.py:16
  384.7 6.8 %multiply_convert_fusion.2 = (bf16[2,32,14,352]{3,1,2,0:T(8,128)(2,1)S(1)}, bf16[2,32,14,352]{3,1,2,0:T(8,128)(2,1)S(1)}) fusion(f32[1,32,14,352]{3,1,2,0:T(8,128)} %copy-done.13, f32[1,32,14,352]{3,1,2,0:T(8,128)} %copy-done.14, f32[1,32,14,352]{3,1,2,0:T(8,128)} %copy-done.12, f32[1,32,14,352]{3,1,2,0:T(8,128)S(1)} %copy-done.11, ...), kind=kOutput, calls=%fused_computation.34 | convolution fusion | flops 1309552640 | bytes 10338305 | tf_op jit(solution)/shard_map/escd,efd->escf/dot_general | solution.py:232
  391.5 4.4 fusion
  396.0 5.7 %add_convert_fusion = bf16[2,32,14,2048]{3,1,2,0:T(8,128)(2,1)} fusion(f32[2,32,14,2048]{3,1,2,0:T(8,128)S(1)} %fusion, bf16[2,32,14,352]{3,1,2,0:T(8,128)(2,1)S(1)} %get-tuple-element.55, bf16[2,2,2048,352]{2,3,1,0:T(8,128)(2,1)} %maximum_select_fusion), kind=kOutput, calls=%fused_computation.10 | convolution fusion | flops 1295515648 | bytes 14524416 | tf_op jit(solution)/shard_map/escf,edf->escd/dot_general | solution.py:238
  402.8 3.9 convolution_bitcast_fusion.1
  412.5 5.6 collective-permute-start.13
  418.0 26.8 %reduce-scatter.5.cloned.1.call-done = bf16[2,32,14,512]{3,1,2,0:T(8,128)(2,1)} async-done(((bf16[2,32,14,2048]{3,1,2,0:T(8,128)(2,1)}), bf16[2,32,14,512]{3,1,2,0:T(8,128)(2,1)}) %reduce-scatter.5.cloned.1.call-update) | async-done | bytes 917520 | tf_op jit(solution)/shard_map/reduce_scatter | solution.py:244
  447.9 9.2 %all-to-all-start.3 = ((bf16[2,32,14,512]{3,0,2,1:T(2,128)(2,1)}), bf16[2,32,14,512]{3,0,2,1:T(2,128)(2,1)S(1)}, u32[]{:S(2)}, u32[]{:S(2)}) async-start(bf16[2,32,14,512]{3,0,2,1:T(2,128)(2,1)} %copy.92), calls=%async_computation.5 | async-start | bytes 1835008 | tf_op jit(solution)/shard_map/all_to_all | solution.py:48
  457.1 4.0 bitcast_convert_fusion
  465.6 35.0 %all-to-all-done.3 = bf16[2,32,14,512]{3,0,2,1:T(2,128)(2,1)S(1)} async-done(((bf16[2,32,14,512]{3,0,2,1:T(2,128)(2,1)}), bf16[2,32,14,512]{3,0,2,1:T(2,128)(2,1)S(1)}, u32[]{:S(2)}, u32[]{:S(2)}) %all-to-all-start.3) | async-done | bytes 917536 | tf_op jit(solution)/shard_map/all_to_all | solution.py:48
  511.6 15.2 %all-reduce.2 = (f32[128]{0:T(128)S(1)}, f32[128,6]{1,0:T(8,128)S(1)}) all-reduce(f32[128]{0:T(128)S(1)} %multiply_reduce_fusion.2, f32[128,6]{1,0:T(8,128)S(1)} %multiply_reduce_fusion), channel_id=1, replica_groups=mesh['dp'=2,'expert'=32,'tensor'=4] {'tensor'}, use_global_device_ids=true, to_apply=%region_11.12 | all-reduce | flops 896 | bytes 7168 | tf_op jit(solution)/shard_map/psum | solution.py:253
  526.9 13.5 %all_gather.7 = bf16[128,2048]{1,0:T(8,128)(2,1)S(1)} all-gather(bf16[128,512]{1,0:T(8,128)(2,1)S(1)} %subtract_convert_fusion), channel_id=1, replica_groups=mesh['dp'=2,'expert'=32,'tensor'=4] {'tensor'}, dimensions={1}, use_global_device_ids=true | all-gather | bytes 655360 | tf_op jit(solution)/shard_map/all_gather | solution.py:261
  541.9 3.4 add_convert_fusion.2
  545.3 5.7 %add_convert_fusion.1 = bf16[2,2,1024,352]{2,3,0,1:T(8,128)(2,1)S(1)} fusion(bf16[2,2,1024,352]{2,3,0,1:T(8,128)(2,1)} %collective-permute-done.13, pred[]{:T(512)S(6)} %eq.46, bf16[2,2,2048,352]{2,3,0,1:T(8,128)(2,1)} %copy-done.1), kind=kLoop, calls=%fused_computation.13 | loop fusion | flops 7208960 | bytes 11534337 | tf_op jit(solution)/shard_map/convert_element_type | solution.py:109
  (162 shorter events, 112.1 us)
Async XLA Ops:
  7.2 140.1 %all-gather.2.cloned.1.call-start = ((), (), s32[]{:S(2)}) async-start(), calls=%async_computation.6 | async-start | bytes 4587520 | tf_op jit(solution)/shard_map/all_gather | solution.py:182
  8.8 7.9 %copy-start.5 = (bf16[2,2,1024,352]{2,3,1,0:T(8,128)(2,1)S(1)}, bf16[2,2,1024,352]{2,3,1,0:T(8,128)(2,1)}, u32[]{:S(2)}) copy-start(bf16[2,2,1024,352]{2,3,1,0:T(8,128)(2,1)} %param.16) | copy-start | bytes 8650756
  8.8 11.2 %copy-start.22 = (s32[128,6]{0,1:T(8,128)S(1)}, s32[128,6]{0,1:T(8,128)}, u32[]{:S(2)}) copy-start(s32[128,6]{0,1:T(8,128)} %param.15) | copy-start | bytes 9220
  11.0 15.1 %collective-permute-start = (bf16[128,512]{1,0:T(8,128)(2,1)}, bf16[128,512]{1,0:T(8,128)(2,1)}, u32[]{:S(2)}, u32[]{:S(2)}) collective-permute-start(bf16[128,512]{1,0:T(8,128)(2,1)} %get-tuple-element.60), channel_id=1, source_target_pairs={{0,1},{1,2},{2,3},{3,0},{4,5},{5,6},{6,7},{7,4},{8,9},{9,10},{10,1... | collective-permute-start | bytes 393224 | tf_op jit(solution)/shard_map/ppermute | solution.py:55
  12.5 13.6 %collective-permute-start.1 = (bf16[128,512]{1,0:T(8,128)(2,1)}, bf16[128,512]{1,0:T(8,128)(2,1)}, u32[]{:S(2)}, u32[]{:S(2)}) collective-permute-start(bf16[128,512]{1,0:T(8,128)(2,1)} %get-tuple-element.59), channel_id=1, source_target_pairs={{0,2},{1,3},{2,0},{3,1},{4,6},{5,7},{6,4},{7,5},{8,10},{9,11},{10,... | collective-permute-start | bytes 393224 | tf_op jit(solution)/shard_map/ppermute | solution.py:55
  15.3 10.9 %collective-permute-start.2 = (bf16[128,512]{1,0:T(8,128)(2,1)S(1)}, bf16[128,512]{1,0:T(8,128)(2,1)}, u32[]{:S(2)}, u32[]{:S(2)}) collective-permute-start(bf16[128,512]{1,0:T(8,128)(2,1)S(1)} %get-tuple-element.58), channel_id=1, source_target_pairs={{0,3},{1,0},{2,1},{3,2},{4,7},{5,4},{6,5},{7,6},{8,11},{9,8},{10,9... | collective-permute-start | bytes 393224 | tf_op jit(solution)/shard_map/ppermute | solution.py:55
  17.9 25.7 %collective-permute-start.4 = (bf16[1,1,1024,352]{2,3,1,0:T(8,128)(2,1)}, bf16[1,1,1024,352]{2,3,1,0:T(8,128)(2,1)S(1)}, u32[]{:S(2)}, u32[]{:S(2)}) collective-permute-start(bf16[1,1,1024,352]{2,3,1,0:T(8,128)(2,1)} %get-tuple-element.54), channel_id=1, source_target_pairs={{0,128},{128,0},{1,129},{129,1},{2,130},{130,2},{3,131},{131,3},{4... | collective-permute-start | bytes 2162696 | tf_op jit(solution)/shard_map/ppermute | solution.py:163
  18.0 48.1 %collective-permute-start.3 = (bf16[2,352,1024]{2,1,0:T(8,128)(2,1)}, bf16[2,352,1024]{2,1,0:T(8,128)(2,1)}, u32[]{:S(2)}, u32[]{:S(2)}) collective-permute-start(bf16[2,352,1024]{2,1,0:T(8,128)(2,1)} %param.17), channel_id=1, source_target_pairs={{0,128},{128,0},{1,129},{129,1},{2,130},{130,2},{3,131},{131,3},{4... | collective-permute-start | bytes 4325384 | tf_op jit(solution)/shard_map/ppermute | solution.py:137
  30.9 4.8 collective-permute-start.5
  31.6 5.1 collective-permute-start.6
  32.5 4.2 collective-permute-start.7
  43.6 105.9 %copy-start.9 = (bf16[1,1,1024,352]{2,3,1,0:T(8,128)(2,1)}, bf16[1,1,1024,352]{2,3,1,0:T(8,128)(2,1)S(1)}, u32[]{:S(2)}) copy-start(bf16[1,1,1024,352]{2,3,1,0:T(8,128)(2,1)S(1)} %collective-permute-done.4) | copy-start | bytes 2162692
  106.4 108.5 %reduce-scatter.3.cloned.1.call-start = ((), (), s32[]{:S(2)}) async-start(), calls=%async_computation.7 | async-start | bytes 4587520 | tf_op jit(solution)/shard_map/reduce_scatter | solution.py:216
  109.0 44.6 %collective-permute-start.8 = (bf16[1,2,1024,352]{2,3,1,0:T(8,128)(2,1)}, bf16[1,2,1024,352]{2,3,1,0:T(8,128)(2,1)}, u32[]{:S(2)}, u32[]{:S(2)}) collective-permute-start(bf16[1,2,1024,352]{2,3,1,0:T(8,128)(2,1)} %slice.107), channel_id=1, source_target_pairs={{0,128},{128,0},{1,129},{129,1},{2,130},{130,2},{3,131},{131,3},{4... | collective-permute-start | bytes 4325384 | tf_op jit(solution)/shard_map/ppermute | solution.py:168
  109.9 48.7 %collective-permute-start.9 = (bf16[1,1,1024,352]{2,3,1,0:T(8,128)(2,1)}, bf16[1,1,1024,352]{2,3,1,0:T(8,128)(2,1)}, u32[]{:S(2)}, u32[]{:S(2)}) collective-permute-start(bf16[1,1,1024,352]{2,3,1,0:T(8,128)(2,1)} %get-tuple-element.53), channel_id=1, source_target_pairs={{0,128},{128,0},{1,129},{129,1},{2,130},{130,2},{3,131},{131,3},{4... | collective-permute-start | bytes 2162696 | tf_op jit(solution)/shard_map/ppermute | solution.py:167
  147.3 4.2 copy-start.6
  151.5 8.8 %copy-start.10 = (f32[1,32,14,352]{3,1,2,0:T(8,128)}, f32[1,32,14,352]{3,1,2,0:T(8,128)S(1)}, u32[]{:S(2)}) copy-start(f32[1,32,14,352]{3,1,2,0:T(8,128)S(1)} %fusion.8) | copy-start | bytes 1892356
  155.4 4.9 copy-start.12
  169.3 58.1 %copy-start.23 = (f32[128,6]{0,1:T(8,128)S(1)}, f32[128,6]{0,1:T(8,128)}, u32[]{:S(2)}) copy-start(f32[128,6]{0,1:T(8,128)} %param.14) | copy-start | bytes 9220
  217.9 32.4 %all-to-all-start.1 = ((bf16[2,32,14,512]{3,0,2,1:T(2,128)(2,1)}), bf16[2,32,14,512]{3,0,2,1:T(2,128)(2,1)}, u32[]{:S(2)}, u32[]{:S(2)}) async-start(bf16[2,32,14,512]{3,0,2,1:T(2,128)(2,1)} %copy.82), calls=%async_computation.2 | async-start | bytes 1835008 | tf_op jit(solution)/shard_map/all_to_all | solution.py:48
  227.0 217.8 %reduce-scatter.5.cloned.1.call-start = ((), (), s32[]{:S(2)}) async-start(), calls=%async_computation.8 | async-start | bytes 4587520 | tf_op jit(solution)/shard_map/reduce_scatter | solution.py:244
  257.4 4.8 copy-start.21
  303.7 24.0 %collective-permute-start.10 = (bf16[2,32,14,512]{3,1,2,0:T(8,128)(2,1)}, bf16[2,32,14,512]{3,1,2,0:T(8,128)(2,1)}, u32[]{:S(2)}, u32[]{:S(2)}) collective-permute-start(bf16[2,32,14,512]{3,1,2,0:T(8,128)(2,1)} %copy.86), channel_id=1, source_target_pairs={{0,1},{1,2},{2,3},{3,0},{4,5},{5,6},{6,7},{7,4},{8,9},{9,10},{10,1... | collective-permute-start | bytes 2752520 | tf_op jit(solution)/shard_map/ppermute | solution.py:27
  304.0 34.0 %collective-permute-start.12 = (bf16[2,32,14,512]{3,1,2,0:T(8,128)(2,1)}, bf16[2,32,14,512]{3,1,2,0:T(8,128)(2,1)S(1)}, u32[]{:S(2)}, u32[]{:S(2)}) collective-permute-start(bf16[2,32,14,512]{3,1,2,0:T(8,128)(2,1)} %copy.86), channel_id=1, source_target_pairs={{1,0},{2,1},{3,2},{0,3},{5,4},{6,5},{7,6},{4,7},{9,8},{10,9},{11,1... | collective-permute-start | bytes 2752520 | tf_op jit(solution)/shard_map/ppermute | solution.py:30
  327.7 23.2 %collective-permute-start.11 = (bf16[2,32,14,512]{3,1,2,0:T(8,128)(2,1)}, bf16[2,32,14,512]{3,1,2,0:T(8,128)(2,1)S(1)}, u32[]{:S(2)}, u32[]{:S(2)}) collective-permute-start(bf16[2,32,14,512]{3,1,2,0:T(8,128)(2,1)} %collective-permute-done.10), channel_id=1, source_target_pairs={{0,1},{1,2},{2,3},{3,0},{4,5},{5,6},{6,7},{7,4},{8,9},{9,10},{10,1... | collective-permute-start | bytes 2752520 | tf_op jit(solution)/shard_map/ppermute | solution.py:27
  377.3 7.4 %copy-start.11 = (f32[1,32,14,352]{3,1,2,0:T(8,128)S(1)}, f32[1,32,14,352]{3,1,2,0:T(8,128)}, u32[]{:S(2)}) copy-start(f32[1,32,14,352]{3,1,2,0:T(8,128)} %copy-done.10) | copy-start | bytes 1892356
  391.5 4.4 copy-start.19
  391.5 4.4 copy-start.16
  412.5 129.4 %collective-permute-start.13 = (bf16[2,2,1024,352]{2,3,0,1:T(8,128)(2,1)}, bf16[2,2,1024,352]{2,3,0,1:T(8,128)(2,1)}, u32[]{:S(2)}, u32[]{:S(2)}) collective-permute-start(bf16[2,2,1024,352]{2,3,0,1:T(8,128)(2,1)} %broadcast_select_fusion), channel_id=1, source_target_pairs={{0,128},{128,0},{1,129},{129,1},{2,130},{130,2},{3,131},{131,3},{4... | collective-permute-start | bytes 8650760 | tf_op jit(solution)/shard_map/ppermute | solution.py:104
  447.9 52.8 %all-to-all-start.3 = ((bf16[2,32,14,512]{3,0,2,1:T(2,128)(2,1)}), bf16[2,32,14,512]{3,0,2,1:T(2,128)(2,1)S(1)}, u32[]{:S(2)}, u32[]{:S(2)}) async-start(bf16[2,32,14,512]{3,0,2,1:T(2,128)(2,1)} %copy.92), calls=%async_computation.5 | async-start | bytes 1835008 | tf_op jit(solution)/shard_map/all_to_all | solution.py:48
  463.9 78.0 %collective-permute-start.14 = (bf16[2,352,1024]{2,1,0:T(8,128)(2,1)}, bf16[2,352,1024]{2,1,0:T(8,128)(2,1)}, u32[]{:S(2)}, u32[]{:S(2)}) collective-permute-start(bf16[2,352,1024]{2,1,0:T(8,128)(2,1)} %broadcast_select_fusion.1), channel_id=1, source_target_pairs={{0,128},{128,0},{1,129},{129,1},{2,130},{130,2},{3,131},{131,3},{4... | collective-permute-start | bytes 4325384 | tf_op jit(solution)/shard_map/ppermute | solution.py:104
  526.7 15.2 %copy-start.4 = (bf16[2,352,2048]{2,1,0:T(8,128)(2,1)S(1)}, bf16[2,352,2048]{2,1,0:T(8,128)(2,1)}, u32[]{:S(2)}) copy-start(bf16[2,352,2048]{2,1,0:T(8,128)(2,1)} %copy-done.3) | copy-start | bytes 8650756
  (12 other events, 29.2 us)
Sparse Core Ops, SparseCore 0:
  106.5 40.7 all-gather.1
  169.5 45.3 reduce-scatter.2
  401.8 42.9 reduce-scatter.4
